TPU v7x, 512 devices: a whole 4x4x16 slice. The times are simulated.
512 devices in a mesh: phase: 16 (over x, z_hi), slab: 32 (over z_lo, y, core).
Axes of the slice: x: 4, y: 4, z: 16 (z_hi: 4, z_lo: 4; z = z_hi * 4 + z_lo), core: 2. Of those that a mesh axis runs over, the one named last changes fastest.
Arguments:
- pressure: float32 [2, 64, 32, 98304], P(None, 'phase', None, 'slab'), may hold values from -6 to 6
- mode_shapes: float32 [1024, 98304], P('phase', 'slab'), may hold values from -0.0390625 to 0.0390625
- point_weight: float32 [98304], P('slab'), may hold values from 0.5 to 2
- panel_order: int32 [8], replicated, may hold values from 0 to 7, each once
Outputs:
- influence: float32 [2, 64, 32, 1024], P(None, None, 'phase', 'slab')
Inputs may be any that keep to these rules, and one draw needn't show every extreme that they name: panel_order names each of 0 to 7 once.
All inputs are finite; a program needn't handle non-finite values.
Results may differ from a plain program's by a relative error of at most 0.00007.
Values sent between devices are 32-bit elements; how exact they have to be, the bound alone decides.
No kernel may reach another device: no remote copies, remote signals or barrier semaphores. Data moves between devices by JAX's collectives and lax.ppermute only.
A program may use at most 64 MiB of HBM per device.

v0:
```python
import math
import jax
import jax.numpy as jnp
from jax import lax
from jax.sharding import PartitionSpec as P


def blade_table(blades, count):
    phases = jnp.arange(count, dtype=jnp.int32)
    target = jnp.arange(blades, dtype=jnp.int32)
    index = target[:, None] * phases[None, :] % blades
    theta = index.astype(jnp.float32) * (2.0 * math.pi / blades)
    cosine = jnp.cos(theta)
    sine = jnp.sin(theta)
    upper = jnp.concatenate([cosine, -sine], axis=1)
    lower = jnp.concatenate([sine, cosine], axis=1)
    return jnp.concatenate([upper, lower], axis=0) * (1.0 / math.sqrt(blades))


def shards(pressure, mode_shapes, point_weight, panel_order):
    weighted = mode_shapes * point_weight[None, :]
    phase_dev = pressure.shape[1]
    excite = pressure.shape[2]
    rows = pressure.reshape(2 * phase_dev * excite, pressure.shape[3])
    partial_forces = lax.dot_general(
        rows,
        lax.all_gather(weighted, "phase", axis=0, tiled=True),
        (((1,), (1,)), ((), ())),
        precision=lax.Precision.HIGHEST,
        preferred_element_type=jnp.float32,
    )
    row_count = partial_forces.shape[0]
    panel_count = panel_order.shape[0]
    panels = partial_forces.reshape(row_count, panel_count, -1)
    selector = (panel_order[:, None] == jnp.arange(panel_count, dtype=jnp.int32)[None, :]).astype(
        jnp.float32
    )
    reordered = jnp.einsum(
        "rqc,pq->rpc", panels, selector, precision=lax.Precision.HIGHEST
    ).reshape(row_count, -1)
    share = lax.psum_scatter(reordered, "slab", scatter_dimension=1, tiled=True)
    mode_local = share.shape[1]
    forces = share.reshape(2, phase_dev, excite, mode_local)
    blades = phase_dev * lax.axis_size("phase")
    gathered = lax.all_to_all(forces, "phase", split_axis=2, concat_axis=1, tiled=True)
    table = blade_table(blades, blades)
    result = jnp.dot(
        table,
        gathered.reshape(2 * blades, -1),
        precision=lax.Precision.HIGHEST,
        preferred_element_type=jnp.float32,
    )
    result = result.reshape(2, blades, -1, mode_local)
    return result


def solution(mesh):
    placed = (P(None, "phase", None, "slab"), P("phase", "slab"), P("slab"), P())
    return jax.shard_map(
        shards,
        mesh=mesh,
        in_specs=placed,
        out_specs=P(None, None, "phase", "slab"),
        check_vma=False,
    )
```

profile of v0, /device:TPU:2, one launch (start us, length us, event | category | flops | bytes accessed | tf_op | source)
XLA Modules:
  0.0 522.7 jit_solution(7747216759934679100)
XLA Ops:
  6.5 0.0 copy-start
  6.5 0.0 copy-start.1
  6.5 0.0 all-gather.2.cloned.1.call-start
  6.5 2.3 broadcast_multiply_fusion
  8.8 0.0 all-gather.2.cloned.1.call-update
  8.8 0.0 reduce-scatter.4.cloned.1.call-start
  8.9 307.7 %all-gather.2.cloned.1.call-done = f32[1024,3072]{1,0:T(8,128)} async-done(((f32[64,3072]{1,0:T(8,128)}), f32[1024,3072]{1,0:T(8,128)}) %all-gather.2.cloned.1.call-update) | async-done | bytes 12582928 | tf_op jit(solution)/shard_map/all_gather | solution.py:27
  316.6 0.0 copy-done
  316.6 13.5 %fusion.12 = f32[1024,256]{1,0:T(8,128)} fusion(f32[1024,3072]{1,0:T(8,128)} %all-gather.2.cloned.1.call-done, f32[256,3072]{1,0:T(8,128)S(1)} %bitcast.35), kind=kOutput, calls=%fused_computation.19 | convolution fusion | flops 9663676416 | bytes 16777216 | tf_op jit(solution)/shard_map/dot_general | solution.py:25
  330.1 2.5 copy.12
  332.6 0.0 copy-done.1
  332.6 2.9 convolution_bitcast_fusion
  335.5 2.5 copy.20
  338.0 0.0 reduce-scatter.4.cloned.1.call-update
  338.1 0.1 fusion.6
  338.2 147.6 %reduce-scatter.4.cloned.1.call-done = f32[32,256]{1,0:T(8,128)} async-done(((f32[1024,256]{1,0:T(8,128)}), f32[32,256]{1,0:T(8,128)}) %reduce-scatter.4.cloned.1.call-update) | async-done | bytes 32784
  485.8 0.9 copy.19
  486.7 0.1 copy.22
  486.8 0.8 reshape.39
  487.5 12.2 %all-to-all-start = ((f32[16,1,512]{2,1,0:T(1,128)}), f32[16,1,512]{2,1,0:T(1,128)S(1)}, u32[]{:S(2)}, u32[]{:S(2)}) async-start(f32[16,1,512]{2,1,0:T(1,128)} %reshape.39), calls=%async_computation | async-start | bytes 65536 | tf_op jit(solution)/shard_map/all_to_all | solution.py:45
  499.8 0.1 fusion.8
  499.9 0.1 maximum_multiply_fusion
  500.0 13.2 %all-to-all-done = f32[16,1,512]{2,1,0:T(1,128)S(1)} async-done(((f32[16,1,512]{2,1,0:T(1,128)}), f32[16,1,512]{2,1,0:T(1,128)S(1)}, u32[]{:S(2)}, u32[]{:S(2)}) %all-to-all-start) | async-done | bytes 32800 | tf_op jit(solution)/shard_map/all_to_all | solution.py:45
  513.2 0.5 broadcast.24
  513.7 0.7 reduce
  514.4 0.1 reshape.40
  514.6 0.1 reshape.33
  514.8 0.1 copy.16
  514.8 1.0 fusion.13
  (2 shorter events, 0.1 us)
Async XLA Ops:
  6.5 310.1 %copy-start = (f32[2,4,32,3072]{3,2,1,0:T(8,128)S(1)}, f32[2,4,32,3072]{3,2,1,0:T(8,128)}, u32[]{:S(2)}) copy-start(f32[2,4,32,3072]{3,2,1,0:T(8,128)} %param.4) | copy-start | bytes 9437188
  6.5 326.1 %copy-start.1 = (s32[8]{0:T(128)S(1)}, s32[8]{0:T(128)}, u32[]{:S(2)}) copy-start(s32[8]{0:T(128)} %param.7) | copy-start | bytes 100
  6.5 310.1 %all-gather.2.cloned.1.call-start = ((), (), s32[]{:S(2)}) async-start(), calls=%async_computation.2 | async-start | bytes 13369344 | tf_op jit(solution)/shard_map/all_gather | solution.py:27
  8.8 477.0 %reduce-scatter.4.cloned.1.call-start = ((), (), s32[]{:S(2)}) async-start(), calls=%async_computation.3 | async-start | bytes 1081344
  487.5 25.7 %all-to-all-start = ((f32[16,1,512]{2,1,0:T(1,128)}), f32[16,1,512]{2,1,0:T(1,128)S(1)}, u32[]{:S(2)}, u32[]{:S(2)}) async-start(f32[16,1,512]{2,1,0:T(1,128)} %reshape.39), calls=%async_computation | async-start | bytes 65536 | tf_op jit(solution)/shard_map/all_to_all | solution.py:45
Sparse Core Ops, SparseCore 0:
  10.4 306.1 all-gather.1
  338.2 147.6 reduce-scatter.3
where the time goes:
time: 523 us
  waiting for transfers between devices  469 us (90%)
  matrix products  17.3 us (3%)
  between operations  13.5 us (3%)
  starting transfers between devices  12.2 us (2%)
  local copies, waits for them, and re-layouts  7.67 us (1%)
    all_gather x1, waiting for transfers between devices, shards(): lax.all_gather(weighted, 'phase', axis=0, tiled=True)  308 us
    unnamed x3, waiting for transfers between devices  148 us
    dot_general x1, matrix products, shards(): lax.dot_general(rows, lax.all_gather(weighted, 'phase', axis=0, tiled=Tru...  13.5 us
    all_to_all x1, waiting for transfers between devices, shards(): lax.all_to_all(forces, 'phase', split_axis=2, concat_axis=1, tiled=True)  13.2 us
    all_to_all x1, starting transfers between devices, shards(): lax.all_to_all(forces, 'phase', split_axis=2, concat_axis=1, tiled=True)  12.2 us
  transfers between devices with their start and end apart: 3, of which 3 were waited for; matrix products, arithmetic and copies ran while one was open for 0% of the time, Pallas kernels for 0%

commit v1 on v0

--- a/solution.py
+++ b/solution.py
@@ -3,6 +3,13 @@
 import jax.numpy as jnp
 from jax import lax
 from jax.sharding import PartitionSpec as P
+
+
+def create_the_side(z_in, axis_tag):
+    latest = jnp.concatenate(
+        jax.lax.all_to_all(jnp.stack(jax.lax.psum(1, axis_tag) * [z_in], 0), axis_tag, 0, 0), 0
+    )
+    return latest
 
 
 def blade_table(blades, count):
@@ -24,7 +31,7 @@
     rows = pressure.reshape(2 * phase_dev * excite, pressure.shape[3])
     partial_forces = lax.dot_general(
         rows,
-        lax.all_gather(weighted, "phase", axis=0, tiled=True),
+        create_the_side(weighted, "phase"),
         (((1,), (1,)), ((), ())),
         precision=lax.Precision.HIGHEST,
         preferred_element_type=jnp.float32,

time: 523 us -> 776 us (1.48)
  blocking collectives: 0 us -> 564 us
  waiting for transfers between devices: 469 us -> 159 us
    all_to_all x0 -> x1, blocking collectives: none -> 564 us  [create_the_side(): jax.lax.all_to_all(jnp.stack(jax.lax.psum(1, axis_tag) * [z_in], 0), axis...]
    all_gather x1 -> x0, waiting for transfers between devices: 308 us -> none  [shards(): lax.all_gather(weighted, 'phase', axis=0, tiled=True)]
    unnamed x3 -> x2, waiting for transfers between devices: 148 us -> 146 us
  transfers between devices with their start and end apart: 3 -> 2, of which waited for: 3 -> 2; matrix products, arithmetic and copies ran while one was open for 0% -> 0% of each run, Pallas kernels for 0% -> 0%
where the time goes in v1:
time: 776 us
  blocking collectives  564 us (73%)
  waiting for transfers between devices  159 us (20%)
  matrix products  15.1 us (2%)
  between operations  13.5 us (2%)
  starting transfers between devices  12.9 us (2%)
  local copies, waits for them, and re-layouts  9.23 us (1%)
    all_to_all x1, blocking collectives, create_the_side(): jax.lax.all_to_all(jnp.stack(jax.lax.psum(1, axis_tag) * [z_in], 0), axis...  564 us
    unnamed x2, waiting for transfers between devices  146 us
  transfers between devices with their start and end apart: 2, of which 2 were waited for; matrix products, arithmetic and copies ran while one was open for 0% of the time, Pallas kernels for 0%

profile of v1, /device:TPU:2, one launch (start us, length us, event | category | flops | bytes accessed | tf_op | source)
XLA Modules:
  0.0 775.8 jit_solution(9211817756864416732)
XLA Ops:
  6.5 0.0 copy-start
  6.5 0.0 reduce-scatter.4.cloned.1.call-start
  6.5 1.3 broadcast_multiply_fusion
  7.9 1.6 stack.2
  9.5 563.7 %all_to_all.20 = f32[16,64,3072]{2,1,0:T(8,128)S(1)} all-to-all(f32[16,64,3072]{2,1,0:T(8,128)S(1)} %stack.2), channel_id=1, replica_groups=mesh['phase'=16,'slab'=32] {'phase'}, dimensions={0} | all-to-all | bytes 25165824 | tf_op jit(solution)/shard_map/all_to_all | solution.py:10
  573.2 0.0 copy-start.1
  573.2 0.0 copy-done
  573.2 11.2 %fusion.12 = f32[1024,256]{1,0:T(8,128)} fusion(f32[1024,3072]{1,0:T(8,128)S(1)} %bitcast.37, f32[256,3072]{1,0:T(8,128)S(1)} %bitcast.36), kind=kOutput, calls=%fused_computation.19 | convolution fusion | flops 9663676416 | bytes 16777216 | tf_op jit(solution)/shard_map/dot_general | solution.py:32
  584.4 2.5 copy.12
  587.0 0.0 copy-done.1
  587.0 2.9 convolution_bitcast_fusion
  589.9 2.5 copy.20
  592.4 0.0 reduce-scatter.4.cloned.1.call-update
  592.4 0.1 fusion.6
  592.6 145.7 %reduce-scatter.4.cloned.1.call-done = f32[32,256]{1,0:T(8,128)} async-done(((f32[1024,256]{1,0:T(8,128)}), f32[32,256]{1,0:T(8,128)}) %reduce-scatter.4.cloned.1.call-update) | async-done | bytes 32784
  738.2 0.9 copy.19
  739.1 0.1 copy.22
  739.2 0.8 reshape.45
  739.9 12.9 %all-to-all-start.1 = ((f32[16,1,512]{2,1,0:T(1,128)}), f32[16,1,512]{2,1,0:T(1,128)S(1)}, u32[]{:S(2)}, u32[]{:S(2)}) async-start(f32[16,1,512]{2,1,0:T(1,128)} %reshape.45), calls=%async_computation.1 | async-start | bytes 65536 | tf_op jit(solution)/shard_map/all_to_all | solution.py:52
  752.9 0.1 fusion.8
  753.0 0.1 maximum_multiply_fusion
  753.1 13.2 %all-to-all-done.1 = f32[16,1,512]{2,1,0:T(1,128)S(1)} async-done(((f32[16,1,512]{2,1,0:T(1,128)}), f32[16,1,512]{2,1,0:T(1,128)S(1)}, u32[]{:S(2)}, u32[]{:S(2)}) %all-to-all-start.1) | async-done | bytes 32800 | tf_op jit(solution)/shard_map/all_to_all | solution.py:52
  766.3 0.5 broadcast.26
  766.8 0.7 reduce
  767.6 0.1 reshape.46
  767.8 0.1 reshape.39
  767.9 0.1 copy.16
  768.0 1.0 fusion.13
  (2 shorter events, 0.1 us)
Async XLA Ops:
  6.5 566.7 %copy-start = (f32[2,4,32,3072]{3,2,1,0:T(8,128)S(1)}, f32[2,4,32,3072]{3,2,1,0:T(8,128)}, u32[]{:S(2)}) copy-start(f32[2,4,32,3072]{3,2,1,0:T(8,128)} %param.4) | copy-start | bytes 9437188
  6.5 731.7 %reduce-scatter.4.cloned.1.call-start = ((), (), s32[]{:S(2)}) async-start(), calls=%async_computation.3 | async-start | bytes 1081344
  573.2 13.8 %copy-start.1 = (s32[8]{0:T(128)S(1)}, s32[8]{0:T(128)}, u32[]{:S(2)}) copy-start(s32[8]{0:T(128)} %param.7) | copy-start | bytes 100
  739.9 26.4 %all-to-all-start.1 = ((f32[16,1,512]{2,1,0:T(1,128)}), f32[16,1,512]{2,1,0:T(1,128)S(1)}, u32[]{:S(2)}, u32[]{:S(2)}) async-start(f32[16,1,512]{2,1,0:T(1,128)} %reshape.45), calls=%async_computation.1 | async-start | bytes 65536 | tf_op jit(solution)/shard_map/all_to_all | solution.py:52
Sparse Core Ops, SparseCore 0:
  592.5 145.6 reduce-scatter.3
